TPU v7x, 512 devices: a whole 4x8x8 slice. The times are simulated.
512 devices in a mesh: req: 64 (over x, y, core), tp: 8 (over z).
Axes of the slice: x: 4, y: 8, z: 8, core: 2. Of those that a mesh axis runs over, the one named last changes fastest.
Arguments:
- vit_context: bfloat16 [32768, 4096], P('req', 'tp'), may hold values from -6 to 6
- vision_residual: bfloat16 [32768, 4096], P('req', 'tp'), may hold values from -75 to 75
- out_weight: bfloat16 [4096, 4096], P('tp', 'req'), may hold values from -0.09375 to 0.09375
- layer_scale: float32 [4096], P('tp'), may hold values from 0.2 to 2
- prompt: bfloat16 [64, 256, 4096], P('req', None, 'tp'), may hold values from -75 to 75
- prompt_len: int32 [64], P('req'), may hold values from 128 to 256
- image_at: int32 [64], P('req'), may hold values from 0 to 128
- grid_sizes: int32 [128, 2], replicated, may hold values from 7 to 8, as said below
- image_owner: int32 [128], replicated, may hold values from 0 to 63, as said below
- norm_gain: float32 [4096], replicated, may hold values from 0.5 to 1.5
- qkv_weight: bfloat16 [4096, 6144], P('req', 'tp'), may hold values from -0.09375 to 0.09375
Outputs:
- qkv: bfloat16 [24576, 6144], P('req', 'tp')
Inputs may be any that keep to these rules, and one draw needn't show every extreme that they name: `image_owner`: each request owns exactly 2 images. `grid_sizes`: each side is 7 or 8; in every draw the images of some request are all 8 by 8, so that request has exactly 128 merged rows.
All inputs are finite; a program needn't handle non-finite values.
Results may differ from a plain program's by a relative error of at most 0.008.
Values may be sent and summed in bfloat16 or wider, within the bound.
No kernel may reach another device: no remote copies, remote signals or barrier semaphores. Data moves between devices by JAX's collectives and lax.ppermute only.
A program may use at most 64 MiB of HBM per device.

v0:
```python
import jax
import jax.numpy as jnp
from jax import lax
from jax.sharding import PartitionSpec as P

HEAD = 128
GROUP = 4
IMG_MAX = 128


def request_plan(grid_sizes, image_owner, requests):
    image_rows = grid_sizes[:, 0] * grid_sizes[:, 1]
    member = (image_owner[:, None] == jnp.arange(requests, dtype=jnp.int32)[None, :]).astype(
        jnp.int32
    )
    counts = jnp.sum(image_rows[:, None] * member, axis=0)
    starts = jnp.cumsum(counts) - counts
    return (counts, starts)


def rope_tables(count):
    half_size = HEAD // 2
    exponent = jnp.arange(half_size, dtype=jnp.float32) * (2.0 / HEAD)
    frequency = jnp.exp(-exponent * jnp.log(jnp.float32(500000.0)))
    angles = jnp.arange(count, dtype=jnp.float32)[:, None] * frequency[None, :]
    return (jnp.cos(angles), jnp.sin(angles))


def apply_rope(projected, cosine_table, sine_table):
    seq_rows = projected.shape[0]
    head_blocks = projected.reshape(seq_rows, -1, GROUP + 2, HEAD)
    turning = head_blocks[:, :, : GROUP + 1, :]
    first_half = turning[..., : HEAD // 2]
    second_half = turning[..., HEAD // 2 :]
    cosine_wide = cosine_table[:, None, None, :]
    sine_wide = sine_table[:, None, None, :]
    turned = jnp.concatenate(
        [
            first_half * cosine_wide - second_half * sine_wide,
            second_half * cosine_wide + first_half * sine_wide,
        ],
        axis=-1,
    )
    head_blocks = jnp.concatenate([turned, head_blocks[:, :, GROUP + 1 :, :]], axis=2)
    return head_blocks.reshape(seq_rows, -1)


def normalize(embedded, norm_gain):
    values = embedded.astype(jnp.float32)
    mean_square = jnp.mean(values * values, axis=-1, keepdims=True)
    return (values * lax.rsqrt(mean_square + 1e-05) * norm_gain[None, :]).astype(jnp.bfloat16)


def shards(
    vit_context,
    vision_residual,
    out_weight,
    layer_scale,
    prompt,
    prompt_len,
    image_at,
    grid_sizes,
    image_owner,
    norm_gain,
    qkv_weight,
):
    requests = lax.axis_size("req")
    device_index = lax.axis_index("req")
    feature_width = vit_context.shape[1]
    merged_context = jnp.mean(
        vit_context.astype(jnp.float32).reshape(-1, 4, feature_width), axis=1
    ).astype(jnp.bfloat16)
    merged_residual = jnp.mean(
        vision_residual.astype(jnp.float32).reshape(-1, 4, feature_width), axis=1
    )
    partial_value = jnp.dot(
        merged_context,
        lax.all_gather(out_weight, "req", axis=1, tiled=True),
        preferred_element_type=jnp.float32,
    )
    summed = lax.psum(partial_value.astype(jnp.bfloat16), "tp").astype(jnp.float32)
    own_share = lax.dynamic_slice_in_dim(
        summed, lax.axis_index("tp") * feature_width, feature_width, 1
    )
    merged = (merged_residual + layer_scale[None, :] * own_share).astype(jnp.bfloat16)
    merged_count = merged.shape[0]
    counts, starts = request_plan(grid_sizes, image_owner, requests)
    request_ends = starts + counts
    capacity = (IMG_MAX + requests - 1) // requests
    request_ids = jnp.arange(requests, dtype=jnp.int32)
    group_index = jnp.arange(merged_count, dtype=jnp.int32) * requests + device_index
    destination = jnp.sum((request_ends[None, :] <= group_index[:, None]).astype(jnp.int32), axis=1)
    owned_start = jnp.sum(
        jnp.where(destination[:, None] == request_ids[None, :], starts[None, :], 0), axis=1
    )
    target = destination * capacity + (group_index - owned_start) // requests
    usable = destination < requests
    send_slots = jnp.arange(requests * capacity, dtype=jnp.int32)
    placing = ((send_slots[:, None] == target[None, :]) & usable[None, :]).astype(jnp.bfloat16)
    outgoing = jnp.dot(placing, merged, preferred_element_type=jnp.float32).astype(jnp.bfloat16)
    arrived = lax.all_to_all(
        outgoing.reshape(requests, capacity, feature_width),
        "req",
        split_axis=0,
        concat_axis=0,
        tiled=True,
    )
    arrived = arrived.reshape(requests * capacity, feature_width)
    own_request = request_ids == device_index
    own_count = jnp.sum(jnp.where(own_request, counts, 0))
    own_start = jnp.sum(jnp.where(own_request, starts, 0))
    image_from = image_at[0]
    prompt_count = prompt_len[0]
    seq_slots = prompt.shape[1] + IMG_MAX
    slot_index = jnp.arange(seq_slots, dtype=jnp.int32)
    image_row = slot_index - image_from
    in_image = (image_row >= 0) & (image_row < own_count)
    is_live = slot_index < prompt_count + own_count
    from_prompt = is_live & jnp.logical_not(in_image)
    flat_index = (own_start + image_row) % requests * capacity + image_row // requests
    image_pick = ((flat_index[:, None] == send_slots[None, :]) & in_image[:, None]).astype(
        jnp.bfloat16
    )
    prompt_row = jnp.where(slot_index < image_from, slot_index, slot_index - own_count)
    prompt_ids = jnp.arange(prompt.shape[1], dtype=jnp.int32)
    prompt_pick = ((prompt_row[:, None] == prompt_ids[None, :]) & from_prompt[:, None]).astype(
        jnp.bfloat16
    )
    embedded = (
        jnp.dot(image_pick, arrived, preferred_element_type=jnp.float32)
        + jnp.dot(prompt_pick, prompt[0], preferred_element_type=jnp.float32)
    ).astype(jnp.bfloat16)
    gathered = lax.all_gather(embedded, "tp", axis=1, tiled=True)
    normed = normalize(gathered, norm_gain)
    projected = jnp.dot(
        normed,
        lax.all_gather(qkv_weight, "req", axis=0, tiled=True),
        preferred_element_type=jnp.float32,
    )
    cosine_table, sine_table = rope_tables(seq_slots)
    return apply_rope(projected, cosine_table, sine_table).astype(jnp.bfloat16)


def solution(mesh):
    in_specs = (
        P("req", "tp"),
        P("req", "tp"),
        P("tp", "req"),
        P("tp"),
        P("req", None, "tp"),
        P("req"),
        P("req"),
        P(),
        P(),
        P(),
        P("req", "tp"),
    )
    out_specs = P("req", "tp")
    return jax.shard_map(shards, mesh=mesh, in_specs=in_specs, out_specs=out_specs, check_vma=False)
```

profile of v0, /device:TPU:1, one launch (start us, length us, event | category | flops | bytes accessed | tf_op | source)
XLA Modules:
  0.0 352.9 jit_solution(7770393168710454331)
XLA Ops:
  6.5 0.7 all-gather.4.cloned.1.call-update
  7.3 1.4 reshape.205
  8.7 0.6 reduce_sum.78
  9.3 0.8 multiply_bitcast_fusion
  10.1 91.0 %all-gather.4.cloned.1.call-done = bf16[512,4096]{0,1:T(8,128)(2,1)} async-done(((bf16[512,64]{0,1:T(8,128)(2,1)}), bf16[512,4096]{0,1:T(8,128)(2,1)}) %all-gather.4.cloned.1.call-update) | async-done | bytes 4194320 | tf_op jit(solution)/shard_map/all_gather | solution.py:78
  101.1 4.6 %convolution_convert_fusion = bf16[128,4096]{1,0:T(8,128)(2,1)} fusion(bf16[512,4096]{0,1:T(8,128)(2,1)} %all-gather.4.cloned.1.call-done, f32[128,512]{1,0:T(8,128)S(1)} %reduce_sum.78), kind=kOutput, calls=%fused_computation.5 | convolution fusion | flops 537526272 | bytes 5505024 | tf_op jit(solution)/shard_map/dot_general | solution.py:76
  105.7 0.1 select_reduce_fusion.1
  105.8 0.1 copy.16
  105.9 0.1 reduce-window.7
  106.0 0.1 reduce
  106.2 0.3 reshape.203
  106.5 0.6 reduce_sum.77
  107.2 0.1 convert_reduce_fusion
  107.3 0.7 fusion.38
  108.0 0.1 select_reduce_fusion
  108.1 73.3 %all-reduce.2.cloned.1.call-done = bf16[128,4096]{1,0:T(8,128)(2,1)} async-done(((bf16[128,4096]{1,0:T(8,128)(2,1)}), bf16[128,4096]{1,0:T(8,128)(2,1)}) %all-reduce.2.cloned.1.call-update) | async-done | bytes 1048592 | tf_op jit(solution)/shard_map/psum | solution.py:81
  181.4 1.1 convolution_convert_fusion.1
  182.5 0.7 reshape.199
  183.3 14.2 %all-to-all-start = ((bf16[64,2,512]{2,1,0:T(2,128)(2,1)}), bf16[64,2,512]{2,1,0:T(2,128)(2,1)S(1)}, u32[]{:S(2)}, u32[]{:S(2)}) async-start(bf16[64,2,512]{2,1,0:T(2,128)(2,1)} %reshape.199), calls=%async_computation | async-start | bytes 262144 | tf_op jit(solution)/shard_map/all_to_all | solution.py:101
  199.3 0.6 fusion.37
  199.9 1.3 fusion.30
  201.2 6.6 %all-to-all-done = bf16[64,2,512]{2,1,0:T(2,128)(2,1)S(1)} async-done(((bf16[64,2,512]{2,1,0:T(2,128)(2,1)}), bf16[64,2,512]{2,1,0:T(2,128)(2,1)S(1)}, u32[]{:S(2)}, u32[]{:S(2)}) %all-to-all-start) | async-done | bytes 131104 | tf_op jit(solution)/shard_map/all_to_all | solution.py:101
  207.9 0.3 fusion.14
  208.2 1.1 fusion.7
  209.3 0.5 all-gather.8.cloned.1.call-update
  209.9 0.4 fusion.21
  210.3 40.0 %all-gather.6.cloned.1.call-done = bf16[384,4096]{1,0:T(8,128)(2,1)} async-done(((bf16[384,512]{1,0:T(8,128)(2,1)}), bf16[384,4096]{1,0:T(8,128)(2,1)}) %all-gather.6.cloned.1.call-update) | async-done | bytes 3145744 | tf_op jit(solution)/shard_map/all_gather | solution.py:133
  250.3 2.6 fusion
  252.9 85.4 %all-gather.8.cloned.1.call-done = bf16[4096,768]{1,0:T(8,128)(2,1)} async-done(((bf16[64,768]{1,0:T(8,128)(2,1)}), bf16[4096,768]{1,0:T(8,128)(2,1)}) %all-gather.8.cloned.1.call-update) | async-done | bytes 6291472 | tf_op jit(solution)/shard_map/all_gather | solution.py:137
  338.3 6.7 %fusion.3 = f32[384,768]{0,1:T(8,128)S(1)} fusion(bf16[4096,768]{1,0:T(8,128)(2,1)} %all-gather.8.cloned.1.call-done, bf16[384,4096]{1,0:T(8,128)(2,1)} %all-gather.6.cloned.1.call-done, f32[4096]{0:T(1024)S(1)} %copy-done.3, f32[384]{0:T(512)S(1)} %add_rsqrt_fusion), kind=kOutput, calls=%fused_computation.6 | convolution fusion | flops 2422210560 | bytes 10634752 | tf_op jit(solution)/shard_map/dot_general | solution.py:135
  345.0 0.1 subtract_convert_fusion
  345.2 1.1 copy.18
  (24 shorter events, 0.4 us)
Async XLA Ops:
  6.5 201.7 %copy-start = (bf16[1,256,512]{2,1,0:T(8,128)(2,1)S(1)}, bf16[1,256,512]{2,1,0:T(8,128)(2,1)}, u32[]{:S(2)}) copy-start(bf16[1,256,512]{2,1,0:T(8,128)(2,1)} %param.15) | copy-start | bytes 786436
  6.5 94.5 %all-gather.4.cloned.1.call-start = ((), (), s32[]{:S(2)}) async-start(), calls=%async_computation.1 | async-start | bytes 4259840 | tf_op jit(solution)/shard_map/all_gather | solution.py:78
  7.3 174.2 %all-reduce.2.cloned.1.call-start = ((), (), s32[]{:S(2)}) async-start(), calls=%async_computation.2 | async-start | bytes 2097152 | tf_op jit(solution)/shard_map/psum | solution.py:81
  8.7 97.0 %copy-start.4 = (s32[128]{0:T(128)S(1)}, s32[128]{0:T(128)}, u32[]{:S(2)}) copy-start(s32[128]{0:T(128)} %param.19) | copy-start | bytes 1540
  8.7 97.5 %copy-start.1 = (bf16[512,512]{1,0:T(8,128)(2,1)S(1)}, bf16[512,512]{1,0:T(8,128)(2,1)}, u32[]{:S(2)}) copy-start(bf16[512,512]{1,0:T(8,128)(2,1)} %param.12) | copy-start | bytes 1572868
  10.1 171.3 %copy-start.2 = (f32[512]{0:T(512)S(1)}, f32[512]{0:T(512)}, u32[]{:S(2)}) copy-start(f32[512]{0:T(512)} %param.14) | copy-start | bytes 6148
  106.5 231.8 %copy-start.3 = (f32[4096]{0:T(1024)S(1)}, f32[4096]{0:T(1024)}, u32[]{:S(2)}) copy-start(f32[4096]{0:T(1024)} %param.20) | copy-start | bytes 49156
  183.3 24.5 %all-to-all-start = ((bf16[64,2,512]{2,1,0:T(2,128)(2,1)}), bf16[64,2,512]{2,1,0:T(2,128)(2,1)S(1)}, u32[]{:S(2)}, u32[]{:S(2)}) async-start(bf16[64,2,512]{2,1,0:T(2,128)(2,1)} %reshape.199), calls=%async_computation | async-start | bytes 262144 | tf_op jit(solution)/shard_map/all_to_all | solution.py:101
  197.4 52.9 %all-gather.6.cloned.1.call-start = ((), (), s32[]{:S(2)}) async-start(), calls=%async_computation.3 | async-start | bytes 3538944 | tf_op jit(solution)/shard_map/all_gather | solution.py:133
  209.3 129.0 %all-gather.8.cloned.1.call-start = ((), (), s32[]{:S(2)}) async-start(), calls=%async_computation.4 | async-start | bytes 6389760 | tf_op jit(solution)/shard_map/all_gather | solution.py:137
Sparse Core Ops, SparseCore 0:
  10.7 90.2 all-gather.3
  105.8 75.5 all-reduce.1
  209.4 40.8 all-gather.5
  253.5 84.7 all-gather.7
where the time goes:
time: 353 us
  waiting for transfers between devices  298 us (84%)
  between operations  15.2 us (4%)
  starting transfers between devices  14.3 us (4%)
  matrix products  13.8 us (4%)
  other arithmetic  8.27 us (2%)
  local copies, waits for them, and re-layouts  3.69 us (1%)
    all_gather x1, waiting for transfers between devices, shards(): lax.all_gather(out_weight, 'req', axis=1, tiled=True)  91 us
    all_gather x1, waiting for transfers between devices, shards(): lax.all_gather(qkv_weight, 'req', axis=0, tiled=True)  85.4 us
    psum x1, waiting for transfers between devices, shards(): lax.psum(partial_value.astype(jnp.bfloat16), 'tp').astype(jnp.float32)  73.3 us
    all_gather x1, waiting for transfers between devices, shards(): gathered = lax.all_gather(embedded, 'tp', axis=1, tiled=True)  40 us
    all_to_all x1, starting transfers between devices, shards(): lax.all_to_all(outgoing.reshape(requests, capacity, feature_width), 'req'...  14.2 us
  transfers between devices with their start and end apart: 5, of which 5 were waited for; matrix products, arithmetic and copies ran while one was open for 3% of the time, Pallas kernels for 0%

commit v1 on v0

--- a/solution.py
+++ b/solution.py
@@ -6,6 +6,19 @@
 HEAD = 128
 GROUP = 4
 IMG_MAX = 128
+
+
+def ring_gather(x, axis, dim):
+    ways = lax.axis_size(axis)
+    up = [(d, (d + 1) % ways) for d in range(ways)]
+    down = [(d, (d - 1) % ways) for d in range(ways)]
+    earlier, later = ([x], [x])
+    for _ in range(ways // 2):
+        earlier.append(lax.ppermute(earlier[-1], axis, up))
+    for _ in range((ways - 1) // 2):
+        later.append(lax.ppermute(later[-1], axis, down))
+    line = jnp.concatenate([*earlier[::-1], *later[1:]], axis=dim)
+    return jnp.roll(line, (lax.axis_index(axis) - ways // 2) * x.shape[dim], axis=dim)
 
 
 def request_plan(grid_sizes, image_owner, requests):
@@ -130,7 +143,7 @@
         jnp.dot(image_pick, arrived, preferred_element_type=jnp.float32)
         + jnp.dot(prompt_pick, prompt[0], preferred_element_type=jnp.float32)
     ).astype(jnp.bfloat16)
-    gathered = lax.all_gather(embedded, "tp", axis=1, tiled=True)
+    gathered = ring_gather(embedded, "tp", 1)
     normed = normalize(gathered, norm_gain)
     projected = jnp.dot(
         normed,

time: 353 us -> 288 us (0.82)
  waiting for transfers between devices: 298 us -> 210 us
  starting transfers between devices: 14.3 us -> 36.4 us
    all_gather x1, waiting for transfers between devices: 85.4 us -> 10.8 us  [shards(): lax.all_gather(qkv_weight, 'req', axis=0, tiled=True)]
    all_gather x1 -> x0, waiting for transfers between devices: 40 us -> none  [shards(): gathered = lax.all_gather(embedded, 'tp', axis=1, tiled=True)]
    ppermute x0 -> x7, waiting for transfers between devices: none -> 27.1 us  [the longest x4 26.1 us: ring_gather(): earlier.append(lax.ppermute(earlier[-1], axis, up))]
    ppermute x0 -> x7, starting transfers between devices: none -> 22.1 us  [the longest x3 13.7 us: ring_gather(): later.append(lax.ppermute(later[-1], axis, down))]
  transfers between devices with their start and end apart: 5 -> 11, of which waited for: 5 -> 9; matrix products, arithmetic and copies ran while one was open for 3% -> 4% of each run, Pallas kernels for 0% -> 0%
where the time goes in v1:
time: 288 us
  waiting for transfers between devices  210 us (73%)
  starting transfers between devices  36.4 us (13%)
  between operations  15.5 us (5%)
  matrix products  13.1 us (5%)
  local copies, waits for them, and re-layouts  7 us (2%)
  other arithmetic  5.58 us (2%)
    all_gather x1, waiting for transfers between devices, shards(): lax.all_gather(out_weight, 'req', axis=1, tiled=True)  91.7 us
    psum x1, waiting for transfers between devices, shards(): lax.psum(partial_value.astype(jnp.bfloat16), 'tp').astype(jnp.float32)  72.7 us
    ppermute x4, waiting for transfers between devices, ring_gather(): earlier.append(lax.ppermute(earlier[-1], axis, up))  26.1 us
    all_to_all x1, starting transfers between devices, shards(): lax.all_to_all(outgoing.reshape(requests, capacity, feature_width), 'req'...  14.2 us
    ppermute x3, starting transfers between devices, ring_gather(): later.append(lax.ppermute(later[-1], axis, down))  13.7 us
    all_gather x1, waiting for transfers between devices, shards(): lax.all_gather(qkv_weight, 'req', axis=0, tiled=True)  10.8 us
    ppermute x4, starting transfers between devices, ring_gather(): earlier.append(lax.ppermute(earlier[-1], axis, up))  8.41 us
    dot_general x1, matrix products, shards(): jnp.dot(normed, lax.all_gather(qkv_weight, 'req', axis=0, tiled=True), pr...  6.69 us
  transfers between devices with their start and end apart: 11, of which 9 were waited for; matrix products, arithmetic and copies ran while one was open for 4% of the time, Pallas kernels for 0%

profile of v1, /device:TPU:1, one launch (start us, length us, event | category | flops | bytes accessed | tf_op | source)
XLA Modules:
  0.0 287.8 jit_solution(23526176670924935)
XLA Ops:
  6.6 0.7 all-gather.3.cloned.1.call-update
  7.3 1.4 reshape.205
  8.7 0.6 reduce_sum.78
  9.3 91.7 %all-gather.3.cloned.1.call-done = bf16[512,4096]{0,1:T(8,128)(2,1)} async-done(((bf16[512,64]{0,1:T(8,128)(2,1)}), bf16[512,4096]{0,1:T(8,128)(2,1)}) %all-gather.3.cloned.1.call-update) | async-done | bytes 4194320 | tf_op jit(solution)/shard_map/all_gather | solution.py:91
  101.1 4.7 %convolution_convert_fusion = bf16[128,4096]{1,0:T(8,128)(2,1)} fusion(bf16[512,4096]{0,1:T(8,128)(2,1)} %all-gather.3.cloned.1.call-done, f32[128,512]{1,0:T(8,128)S(1)} %reduce_sum.78), kind=kOutput, calls=%fused_computation.5 | convolution fusion | flops 537526272 | bytes 5505024 | tf_op jit(solution)/shard_map/dot_general | solution.py:89
  105.8 0.7 all-gather.5.cloned.1.call-update
  107.3 0.6 reduce_sum.77
  108.0 0.7 fusion.39
  108.8 72.7 %all-reduce.2.cloned.1.call-done = bf16[128,4096]{1,0:T(8,128)(2,1)} async-done(((bf16[128,4096]{1,0:T(8,128)(2,1)}), bf16[128,4096]{1,0:T(8,128)(2,1)}) %all-reduce.2.cloned.1.call-update) | async-done | bytes 1048592 | tf_op jit(solution)/shard_map/psum | solution.py:94
  181.5 1.1 convolution_convert_fusion.1
  182.6 0.7 reshape.199
  183.3 14.2 %all-to-all-start = ((bf16[64,2,512]{2,1,0:T(2,128)(2,1)}), bf16[64,2,512]{2,1,0:T(2,128)(2,1)S(1)}, u32[]{:S(2)}, u32[]{:S(2)}) async-start(bf16[64,2,512]{2,1,0:T(2,128)(2,1)} %reshape.199), calls=%async_computation | async-start | bytes 262144 | tf_op jit(solution)/shard_map/all_to_all | solution.py:114
  199.4 0.6 fusion.38
  200.0 1.2 fusion.31
  201.3 6.6 %all-to-all-done = bf16[64,2,512]{2,1,0:T(2,128)(2,1)S(1)} async-done(((bf16[64,2,512]{2,1,0:T(2,128)(2,1)}), bf16[64,2,512]{2,1,0:T(2,128)(2,1)S(1)}, u32[]{:S(2)}, u32[]{:S(2)}) %all-to-all-start) | async-done | bytes 131104 | tf_op jit(solution)/shard_map/all_to_all | solution.py:114
  208.6 2.7 collective-permute-start
  211.3 10.8 %collective-permute-done = bf16[384,512]{1,0:T(8,128)(2,1)S(1)} collective-permute-done((bf16[384,512]{1,0:T(8,128)(2,1)S(1)}, bf16[384,512]{1,0:T(8,128)(2,1)S(1)}, u32[]{:S(2)}, u32[]{:S(2)}) %collective-permute-start) | collective-permute-done | bytes 393248 | tf_op jit(solution)/shard_map/ppermute | solution.py:17
  222.1 1.9 collective-permute-start.1
  224.0 4.6 %collective-permute-start.4 = (bf16[384,512]{1,0:T(8,128)(2,1)S(1)}, bf16[384,512]{1,0:T(8,128)(2,1)S(1)}, u32[]{:S(2)}, u32[]{:S(2)}) collective-permute-start(bf16[384,512]{1,0:T(8,128)(2,1)S(1)} %fusion.8), channel_id=1, source_target_pairs={{0,7},{1,0},{2,1},{3,2},{4,3},{5,4},{6,5},{7,6},{8,15},{9,8},{10,9... | collective-permute-start | bytes 1179656 | tf_op jit(solution)/shard_map/ppermute | solution.py:19
  228.6 6.1 %collective-permute-done.1 = bf16[384,512]{1,0:T(8,128)(2,1)S(1)} collective-permute-done((bf16[384,512]{1,0:T(8,128)(2,1)S(1)}, bf16[384,512]{1,0:T(8,128)(2,1)S(1)}, u32[]{:S(2)}, u32[]{:S(2)}) %collective-permute-start.1) | collective-permute-done | bytes 393248 | tf_op jit(solution)/shard_map/ppermute | solution.py:17
  234.7 1.9 collective-permute-start.2
  236.6 4.6 %collective-permute-start.5 = (bf16[384,512]{1,0:T(8,128)(2,1)S(1)}, bf16[384,512]{1,0:T(8,128)(2,1)S(1)}, u32[]{:S(2)}, u32[]{:S(2)}) collective-permute-start(bf16[384,512]{1,0:T(8,128)(2,1)S(1)} %collective-permute-done.4), channel_id=1, source_target_pairs={{0,7},{1,0},{2,1},{3,2},{4,3},{5,4},{6,5},{7,6},{8,15},{9,8},{10,9... | collective-permute-start | bytes 1179656 | tf_op jit(solution)/shard_map/ppermute | solution.py:19
  241.2 5.3 %collective-permute-done.2 = bf16[384,512]{1,0:T(8,128)(2,1)S(1)} collective-permute-done((bf16[384,512]{1,0:T(8,128)(2,1)S(1)}, bf16[384,512]{1,0:T(8,128)(2,1)S(1)}, u32[]{:S(2)}, u32[]{:S(2)}) %collective-permute-start.2) | collective-permute-done | bytes 393248 | tf_op jit(solution)/shard_map/ppermute | solution.py:17
  246.4 1.9 collective-permute-start.3
  248.8 4.6 %collective-permute-start.6 = (bf16[384,512]{1,0:T(8,128)(2,1)S(1)}, bf16[384,512]{1,0:T(8,128)(2,1)S(1)}, u32[]{:S(2)}, u32[]{:S(2)}) collective-permute-start(bf16[384,512]{1,0:T(8,128)(2,1)S(1)} %collective-permute-done.5), channel_id=1, source_target_pairs={{0,7},{1,0},{2,1},{3,2},{4,3},{5,4},{6,5},{7,6},{8,15},{9,8},{10,9... | collective-permute-start | bytes 1179656 | tf_op jit(solution)/shard_map/ppermute | solution.py:19
  253.4 4.0 %collective-permute-done.3 = bf16[384,512]{1,0:T(8,128)(2,1)S(1)} collective-permute-done((bf16[384,512]{1,0:T(8,128)(2,1)S(1)}, bf16[384,512]{1,0:T(8,128)(2,1)S(1)}, u32[]{:S(2)}, u32[]{:S(2)}) %collective-permute-start.3) | collective-permute-done | bytes 393248 | tf_op jit(solution)/shard_map/ppermute | solution.py:17
  257.7 0.9 collective-permute-done.6
  259.1 2.7 copy-done.1
  261.8 0.7 fusion
  262.5 10.8 %all-gather.5.cloned.1.call-done = bf16[4096,768]{1,0:T(8,128)(2,1)} async-done(((bf16[64,768]{1,0:T(8,128)(2,1)}), bf16[4096,768]{1,0:T(8,128)(2,1)}) %all-gather.5.cloned.1.call-update) | async-done | bytes 6291472 | tf_op jit(solution)/shard_map/all_gather | solution.py:150
  273.3 6.7 %fusion.3 = f32[384,768]{0,1:T(8,128)S(1)} fusion(bf16[4096,768]{1,0:T(8,128)(2,1)} %all-gather.5.cloned.1.call-done, f32[4096]{0:T(1024)S(1)} %copy-done.4, f32[384]{0:T(512)S(1)} %add_rsqrt_fusion, bf16[384,8192]{1,0:T(8,128)(2,1)} %copy-done.1, s32[]{:T(128)S(6)} %select_n.71), kind=kOutput, calls=%fused_computation.6 | convolution fusion | flops 2422210560 | bytes 10634756 | tf_op jit(solution)/shard_map/dot_general | solution.py:148
  280.2 1.1 copy.18
  (55 shorter events, 3.1 us)
Async XLA Ops:
  6.5 201.7 %copy-start = (bf16[1,256,512]{2,1,0:T(8,128)(2,1)S(1)}, bf16[1,256,512]{2,1,0:T(8,128)(2,1)}, u32[]{:S(2)}) copy-start(bf16[1,256,512]{2,1,0:T(8,128)(2,1)} %param.15) | copy-start | bytes 786436
  6.5 100.0 %copy-start.5 = (s32[128,2]{0,1:T(2,128)S(1)}, s32[128,2]{0,1:T(2,128)}, u32[]{:S(2)}) copy-start(s32[128,2]{0,1:T(2,128)} %param.18) | copy-start | bytes 3076
  6.5 100.0 %copy-start.6 = (s32[128]{0:T(128)S(1)}, s32[128]{0:T(128)}, u32[]{:S(2)}) copy-start(s32[128]{0:T(128)} %param.19) | copy-start | bytes 1540
  6.5 100.4 %copy-start.2 = (bf16[512,512]{1,0:T(8,128)(2,1)S(1)}, bf16[512,512]{1,0:T(8,128)(2,1)}, u32[]{:S(2)}) copy-start(bf16[512,512]{1,0:T(8,128)(2,1)} %param.12) | copy-start | bytes 1572868
  6.5 94.5 %all-gather.3.cloned.1.call-start = ((), (), s32[]{:S(2)}) async-start(), calls=%async_computation.1 | async-start | bytes 4259840 | tf_op jit(solution)/shard_map/all_gather | solution.py:91
  7.3 174.2 %copy-start.3 = (f32[512]{0:T(512)S(1)}, f32[512]{0:T(512)}, u32[]{:S(2)}) copy-start(f32[512]{0:T(512)} %param.14) | copy-start | bytes 6148
  7.3 174.2 %all-reduce.2.cloned.1.call-start = ((), (), s32[]{:S(2)}) async-start(), calls=%async_computation.2 | async-start | bytes 2097152 | tf_op jit(solution)/shard_map/psum | solution.py:94
  105.8 167.5 %all-gather.5.cloned.1.call-start = ((), (), s32[]{:S(2)}) async-start(), calls=%async_computation.3 | async-start | bytes 6389760 | tf_op jit(solution)/shard_map/all_gather | solution.py:150
  183.3 24.5 %all-to-all-start = ((bf16[64,2,512]{2,1,0:T(2,128)(2,1)}), bf16[64,2,512]{2,1,0:T(2,128)(2,1)S(1)}, u32[]{:S(2)}, u32[]{:S(2)}) async-start(bf16[64,2,512]{2,1,0:T(2,128)(2,1)} %reshape.199), calls=%async_computation | async-start | bytes 262144 | tf_op jit(solution)/shard_map/all_to_all | solution.py:114
  208.6 13.5 %collective-permute-start = (bf16[384,512]{1,0:T(8,128)(2,1)S(1)}, bf16[384,512]{1,0:T(8,128)(2,1)S(1)}, u32[]{:S(2)}, u32[]{:S(2)}) collective-permute-start(bf16[384,512]{1,0:T(8,128)(2,1)S(1)} %fusion.8), channel_id=1, source_target_pairs={{0,1},{1,2},{2,3},{3,4},{4,5},{5,6},{6,7},{7,0},{8,9},{9,10},{10,1... | collective-permute-start | bytes 1179656 | tf_op jit(solution)/shard_map/ppermute | solution.py:17
  222.1 12.6 %collective-permute-start.1 = (bf16[384,512]{1,0:T(8,128)(2,1)S(1)}, bf16[384,512]{1,0:T(8,128)(2,1)S(1)}, u32[]{:S(2)}, u32[]{:S(2)}) collective-permute-start(bf16[384,512]{1,0:T(8,128)(2,1)S(1)} %collective-permute-done), channel_id=1, source_target_pairs={{0,1},{1,2},{2,3},{3,4},{4,5},{5,6},{6,7},{7,0},{8,9},{9,10},{10,1... | collective-permute-start | bytes 1179656 | tf_op jit(solution)/shard_map/ppermute | solution.py:17
  224.0 12.6 %collective-permute-start.4 = (bf16[384,512]{1,0:T(8,128)(2,1)S(1)}, bf16[384,512]{1,0:T(8,128)(2,1)S(1)}, u32[]{:S(2)}, u32[]{:S(2)}) collective-permute-start(bf16[384,512]{1,0:T(8,128)(2,1)S(1)} %fusion.8), channel_id=1, source_target_pairs={{0,7},{1,0},{2,1},{3,2},{4,3},{5,4},{6,5},{7,6},{8,15},{9,8},{10,9... | collective-permute-start | bytes 1179656 | tf_op jit(solution)/shard_map/ppermute | solution.py:19
  234.7 11.8 %collective-permute-start.2 = (bf16[384,512]{1,0:T(8,128)(2,1)S(1)}, bf16[384,512]{1,0:T(8,128)(2,1)S(1)}, u32[]{:S(2)}, u32[]{:S(2)}) collective-permute-start(bf16[384,512]{1,0:T(8,128)(2,1)S(1)} %collective-permute-done.1), channel_id=1, source_target_pairs={{0,1},{1,2},{2,3},{3,4},{4,5},{5,6},{6,7},{7,0},{8,9},{9,10},{10,1... | collective-permute-start | bytes 1179656 | tf_op jit(solution)/shard_map/ppermute | solution.py:17
  236.6 12.2 %collective-permute-start.5 = (bf16[384,512]{1,0:T(8,128)(2,1)S(1)}, bf16[384,512]{1,0:T(8,128)(2,1)S(1)}, u32[]{:S(2)}, u32[]{:S(2)}) collective-permute-start(bf16[384,512]{1,0:T(8,128)(2,1)S(1)} %collective-permute-done.4), channel_id=1, source_target_pairs={{0,7},{1,0},{2,1},{3,2},{4,3},{5,4},{6,5},{7,6},{8,15},{9,8},{10,9... | collective-permute-start | bytes 1179656 | tf_op jit(solution)/shard_map/ppermute | solution.py:19
  246.4 10.9 %collective-permute-start.3 = (bf16[384,512]{1,0:T(8,128)(2,1)S(1)}, bf16[384,512]{1,0:T(8,128)(2,1)S(1)}, u32[]{:S(2)}, u32[]{:S(2)}) collective-permute-start(bf16[384,512]{1,0:T(8,128)(2,1)S(1)} %collective-permute-done.2), channel_id=1, source_target_pairs={{0,1},{1,2},{2,3},{3,4},{4,5},{5,6},{6,7},{7,0},{8,9},{9,10},{10,1... | collective-permute-start | bytes 1179656 | tf_op jit(solution)/shard_map/ppermute | solution.py:17
  248.8 9.8 %collective-permute-start.6 = (bf16[384,512]{1,0:T(8,128)(2,1)S(1)}, bf16[384,512]{1,0:T(8,128)(2,1)S(1)}, u32[]{:S(2)}, u32[]{:S(2)}) collective-permute-start(bf16[384,512]{1,0:T(8,128)(2,1)S(1)} %collective-permute-done.5), channel_id=1, source_target_pairs={{0,7},{1,0},{2,1},{3,2},{4,3},{5,4},{6,5},{7,6},{8,15},{9,8},{10,9... | collective-permute-start | bytes 1179656 | tf_op jit(solution)/shard_map/ppermute | solution.py:19
  257.6 15.7 %copy-start.4 = (f32[4096]{0:T(1024)S(1)}, f32[4096]{0:T(1024)}, u32[]{:S(2)}) copy-start(f32[4096]{0:T(1024)} %param.20) | copy-start | bytes 49156
  259.1 2.7 copy-start.1
Sparse Core Ops, SparseCore 0:
  10.7 90.2 all-gather.2
  105.9 75.5 all-reduce.1
  184.8 88.4 all-gather.4
